TPU v7x, 512 devices: a whole 4x4x16 slice. The times are simulated.
512 devices in a mesh: head: 8 (over x, core), expert: 64 (over z, y).
Axes of the slice: x: 4, y: 4, z: 16, core: 2. Of those that a mesh axis runs over, the one named last changes fastest.
Arguments:
- q_latent: bfloat16 [512, 64, 512], P('expert', 'head'), may hold values from -16 to 16
- q_rotary: bfloat16 [512, 64, 64], P('expert', 'head'), may hold values from -3 to 3
- cache_latent: bfloat16 [512, 128, 512], P('expert'), may hold values from -5 to 5
- cache_rotary: bfloat16 [512, 64, 128], P('expert'), may hold values from -5 to 5
- lengths: int32 [512], P('expert'), may hold values from 16 to 128, as said below
- w_value_out: bfloat16 [32768, 5120], P('head', 'expert'), may hold values from -0.25 to 0.25
- resid: bfloat16 [512, 5120], P('expert'), may hold values from -8 to 8
- norm_gain: float32 [5120], replicated, may hold values from 0.1 to 1.9
- route_ids: int32 [512, 6], P('expert'), may hold values from 0 to 63, as said below
- route_weights: float32 [512, 6], P('expert'), may hold values from 0.1 to 0.6
- w_gate_up: bfloat16 [64, 2, 768, 5120], P('expert', None, 'head'), may hold values from -0.078125 to 0.078125
- w_down: bfloat16 [64, 768, 5120], P('expert', 'head'), may hold values from -0.21875 to 0.21875
Outputs:
- mixed_out: float32 [512, 5120], P('expert', 'head')
Inputs may be any that keep to these rules, and one draw needn't show every extreme that they name: `lengths`: slots at positions below a sequence's length are valid; some sequence has length 128. `route_ids`: each row names 6 different experts. Among the rows of one device (aligned blocks of 8 rows) no expert is named by more than 2 rows, and one expert is named by exactly 2 rows in every block.
All inputs are finite; a program needn't handle non-finite values.
Results may differ from a plain program's by a relative error of at most 0.0046.
Values may be sent and summed in bfloat16 or wider, within the bound.
No kernel may reach another device: no remote copies, remote signals or barrier semaphores. Data moves between devices by JAX's collectives and lax.ppermute only.
A program may use at most 64 MiB of HBM per device.

v0:
```python
import jax
import jax.numpy as jnp
from jax import lax
from jax.sharding import PartitionSpec as P

softmax_scale = 192.0 ** (-0.5)
norm_epsilon = 1e-06


def attend(q_latent, q_rotary, cache_latent, cache_rotary, lengths):
    scores = jnp.einsum("shl,scl->shc", q_latent, cache_latent, preferred_element_type=jnp.float32)
    scores = scores + jnp.einsum(
        "shr,src->shc", q_rotary, cache_rotary, preferred_element_type=jnp.float32
    )
    scores = scores * softmax_scale
    position = lax.broadcasted_iota(jnp.int32, scores.shape, 2)
    scores = jnp.where(position < lengths[:, None, None], scores, -1e30)
    highest = jnp.max(scores, axis=2, keepdims=True)
    weights = jnp.exp(scores - highest)
    probs = (weights / jnp.sum(weights, axis=2, keepdims=True)).astype(jnp.bfloat16)
    return jnp.einsum(
        "shc,scl->shl", probs, cache_latent, preferred_element_type=jnp.float32
    ).astype(jnp.bfloat16)


def on_device(
    q_latent,
    q_rotary,
    cache_latent,
    cache_rotary,
    lengths,
    w_value_out,
    resid,
    norm_gain,
    route_ids,
    route_weights,
    w_gate_up,
    w_down,
):
    seq_local = q_latent.shape[0]
    latent_out = attend(q_latent, q_rotary, cache_latent, cache_rotary, lengths)
    flattened = latent_out.reshape(seq_local, -1)
    column_terms = jnp.dot(
        lax.all_gather(flattened, "expert", axis=0, tiled=True),
        w_value_out,
        preferred_element_type=jnp.float32,
    )
    column_sums = lax.psum(column_terms, "head")
    attention = lax.all_to_all(
        column_sums.astype(jnp.bfloat16), "expert", split_axis=0, concat_axis=1, tiled=True
    )
    stream = resid.astype(jnp.float32) + attention.astype(jnp.float32)
    mean_square = jnp.mean(stream * stream, axis=1, keepdims=True)
    normed = (stream * lax.rsqrt(mean_square + norm_epsilon) * norm_gain).astype(jnp.bfloat16)
    expert_count = lax.axis_size("expert")
    top_count = route_ids.shape[1]
    capacity = max(2, -(-(seq_local * top_count) // expert_count))
    flat_ids = route_ids.reshape(-1)
    one_hot = (flat_ids[:, None] == jnp.arange(expert_count, dtype=jnp.int32)[None, :]).astype(
        jnp.int32
    )
    earlier = jnp.cumsum(one_hot, axis=0) - one_hot
    slot_index = jnp.sum(earlier * one_hot, axis=1)
    target = (flat_ids * capacity + slot_index).reshape(seq_local, top_count)
    places = jnp.arange(expert_count * capacity, dtype=jnp.int32)
    matches = target[None, :, :] == places[:, None, None]
    selector = jnp.sum(matches.astype(jnp.int32), axis=2).astype(jnp.bfloat16)
    blending = jnp.sum(jnp.where(matches, route_weights[None, :, :], 0.0), axis=2)
    gate_up = w_gate_up[0]
    down_local = w_down[0]
    col_width = stream.shape[1] // lax.axis_size("head")
    offset = lax.axis_index("head") * col_width
    normed_cols = lax.dynamic_slice_in_dim(normed, offset, col_width, 1)
    outgoing = jnp.dot(selector, normed_cols, preferred_element_type=jnp.float32).astype(
        jnp.bfloat16
    )
    outgoing = outgoing.reshape(expert_count, capacity, -1)
    arrived = lax.all_to_all(outgoing, "expert", split_axis=0, concat_axis=0, tiled=True)
    arrived_cols = arrived.reshape(-1, arrived.shape[2])
    flat_rows = lax.all_gather(arrived_cols, "head", axis=1, tiled=True)
    projected = jnp.einsum("rd,gfd->rgf", flat_rows, gate_up, preferred_element_type=jnp.float32)
    hidden = (jax.nn.silu(projected[:, 0]) * projected[:, 1]).astype(jnp.bfloat16)
    partial_rows = jnp.dot(hidden, down_local, preferred_element_type=jnp.float32)
    summed_cols = lax.psum_scatter(
        partial_rows.astype(jnp.bfloat16), "head", scatter_dimension=1, tiled=True
    )
    summed_rows = summed_cols.reshape(expert_count, capacity, -1)
    returned = lax.all_to_all(summed_rows, "expert", split_axis=0, concat_axis=0, tiled=True)
    back_rows = returned.reshape(expert_count * capacity, -1).astype(jnp.float32)
    mixture = jnp.dot(blending.T, back_rows, precision=lax.Precision.HIGHEST)
    stream_cols = lax.dynamic_slice_in_dim(stream, offset, col_width, 1)
    return stream_cols + mixture


def solution(mesh):
    placed = (
        P("expert", "head", None),
        P("expert", "head", None),
        P("expert", None, None),
        P("expert", None, None),
        P("expert"),
        P("head", "expert"),
        P("expert", None),
        P(),
        P("expert", None),
        P("expert", None),
        P("expert", None, "head", None),
        P("expert", "head", None),
    )
    return jax.shard_map(
        on_device, mesh=mesh, in_specs=placed, out_specs=P("expert", "head"), check_vma=False
    )
```

profile of v0, /device:TPU:7, one launch (start us, length us, event | category | flops | bytes accessed | tf_op | source)
XLA Modules:
  0.0 349.5 jit_solution(5322238232163485525)
XLA Ops:
  6.5 1.8 fusion.21
  8.3 1.1 fusion.8
  9.6 1.5 fusion.4
  11.1 0.7 copy.24
  12.3 142.5 %all-gather.3.cloned.1.call-done = bf16[512,4096]{1,0:T(8,128)(2,1)} async-done(((bf16[8,4096]{1,0:T(8,128)(2,1)}), bf16[512,4096]{1,0:T(8,128)(2,1)}) %all-gather.3.cloned.1.call-update) | async-done | bytes 4194320 | tf_op jit(solution)/shard_map/all_gather | solution.py:44
  154.8 3.6 %fusion.22 = f32[512,80]{0,1:T(8,128)S(1)} fusion(bf16[512,4096]{1,0:T(8,128)(2,1)} %all-gather.3.cloned.1.call-done, bf16[4096,80]{0,1:T(8,128)(2,1)S(1)} %copy-done.1), kind=kOutput, calls=%fused_computation.40 | convolution fusion | flops 335544320 | bytes 5013504 | tf_op jit(solution)/shard_map/dot_general | solution.py:43
  158.4 31.2 %all-reduce.1 = bf16[512,80]{0,1:T(8,128)(2,1)S(1)} all-reduce(f32[512,80]{0,1:T(8,128)S(1)} %fusion.22), channel_id=1, replica_groups=mesh['head'=8,'expert'=64] {'head'}, use_global_device_ids=true, to_apply=%region_2.3 | all-reduce | flops 40960 | bytes 245760 | tf_op jit(solution)/shard_map/psum | solution.py:48
  189.6 0.7 copy.18
  190.4 8.6 %all-to-all-start = ((bf16[64,8,80]{2,1,0:T(8,128)(2,1)}), bf16[64,8,80]{2,1,0:T(8,128)(2,1)S(1)}, u32[]{:S(2)}, u32[]{:S(2)}) async-start(bf16[64,8,80]{2,1,0:T(8,128)(2,1)} %bitcast), calls=%async_computation | async-start | bytes 262144 | tf_op jit(solution)/shard_map/all_to_all | solution.py:49
  199.1 0.8 dynamic-slice
  200.0 15.2 %all-to-all-done = bf16[64,8,80]{2,1,0:T(8,128)(2,1)S(1)} async-done(((bf16[64,8,80]{2,1,0:T(8,128)(2,1)}), bf16[64,8,80]{2,1,0:T(8,128)(2,1)S(1)}, u32[]{:S(2)}, u32[]{:S(2)}) %all-to-all-start) | async-done | bytes 81952 | tf_op jit(solution)/shard_map/all_to_all | solution.py:49
  215.6 0.3 convolution_convert_fusion.1
  216.0 20.6 %all_to_all.23 = bf16[64,2,640]{2,1,0:T(2,128)(2,1)S(1)} all-to-all(bf16[64,2,640]{2,1,0:T(2,128)(2,1)S(1)} %reshape.43), channel_id=1, replica_groups=mesh['head'=8,'expert'=64] {'expert'}, dimensions={0} | all-to-all | bytes 327680 | tf_op jit(solution)/shard_map/all_to_all | solution.py:78
  236.6 0.7 reshape.44
  237.4 24.3 %all-gather.5.cloned.1.call-done = bf16[128,5120]{1,0:T(8,128)(2,1)} async-done(((bf16[128,640]{1,0:T(8,128)(2,1)}), bf16[128,5120]{1,0:T(8,128)(2,1)}) %all-gather.5.cloned.1.call-update) | async-done | bytes 1310736 | tf_op jit(solution)/shard_map/all_gather | solution.py:80
  261.6 2.0 fusion.1
  263.6 1.7 convolution_convert_fusion
  265.4 1.5 copy.22
  266.9 40.3 %reduce-scatter.4.cloned.1.call-done = bf16[640,128]{1,0:T(8,128)(2,1)} async-done(((bf16[5120,128]{1,0:T(8,128)(2,1)}), bf16[640,128]{1,0:T(8,128)(2,1)}) %reduce-scatter.4.cloned.1.call-update) | async-done | bytes 163856
  307.2 1.1 copy.23
  308.2 0.7 reshape.45
  309.0 14.4 %all-to-all-start.2 = ((bf16[64,2,640]{2,1,0:T(2,128)(2,1)}), bf16[64,2,640]{2,1,0:T(2,128)(2,1)S(1)}, u32[]{:S(2)}, u32[]{:S(2)}) async-start(bf16[64,2,640]{2,1,0:T(2,128)(2,1)} %reshape.45), calls=%async_computation.2 | async-start | bytes 327680 | tf_op jit(solution)/shard_map/all_to_all | solution.py:88
  323.6 18.6 %all-to-all-done.2 = bf16[64,2,640]{2,1,0:T(2,128)(2,1)S(1)} async-done(((bf16[64,2,640]{2,1,0:T(2,128)(2,1)}), bf16[64,2,640]{2,1,0:T(2,128)(2,1)S(1)}, u32[]{:S(2)}, u32[]{:S(2)}) %all-to-all-start.2) | async-done | bytes 163872 | tf_op jit(solution)/shard_map/all_to_all | solution.py:88
  342.2 0.8 convolution_add_fusion.1
  (34 shorter events, 1.7 us)
Async XLA Ops:
  6.5 255.1 %copy-start = (bf16[1,2,96,5120]{3,2,1,0:T(8,128)(2,1)S(1)}, bf16[1,2,96,5120]{3,2,1,0:T(8,128)(2,1)}, u32[]{:S(2)}) copy-start(bf16[1,2,96,5120]{3,2,1,0:T(8,128)(2,1)} %param.22) | copy-start | bytes 5898244
  6.5 5.3 %copy-start.3 = (s32[8,6]{1,0:T(8,128)S(1)}, s32[8,6]{1,0:T(8,128)}, u32[]{:S(2)}) copy-start(s32[8,6]{1,0:T(8,128)} %param.20) | copy-start | bytes 580
  6.5 148.3 %copy-start.1 = (bf16[4096,80]{0,1:T(8,128)(2,1)S(1)}, bf16[4096,80]{0,1:T(8,128)(2,1)}, u32[]{:S(2)}) copy-start(bf16[4096,80]{0,1:T(8,128)(2,1)} %param.17) | copy-start | bytes 1966084
  6.5 148.3 %all-gather.3.cloned.1.call-start = ((), (), s32[]{:S(2)}) async-start(), calls=%async_computation.4 | async-start | bytes 4259840 | tf_op jit(solution)/shard_map/all_gather | solution.py:44
  158.4 57.0 %copy-start.2 = (bf16[8,5120]{1,0:T(8,128)(2,1)S(1)}, bf16[8,5120]{1,0:T(8,128)(2,1)}, u32[]{:S(2)}) copy-start(bf16[8,5120]{1,0:T(8,128)(2,1)} %param.18) | copy-start | bytes 245764
  190.4 24.8 %all-to-all-start = ((bf16[64,8,80]{2,1,0:T(8,128)(2,1)}), bf16[64,8,80]{2,1,0:T(8,128)(2,1)S(1)}, u32[]{:S(2)}, u32[]{:S(2)}) async-start(bf16[64,8,80]{2,1,0:T(8,128)(2,1)} %bitcast), calls=%async_computation | async-start | bytes 262144 | tf_op jit(solution)/shard_map/all_to_all | solution.py:49
  199.0 62.6 %all-gather.5.cloned.1.call-start = ((), (), s32[]{:S(2)}) async-start(), calls=%async_computation.5 | async-start | bytes 1474560 | tf_op jit(solution)/shard_map/all_gather | solution.py:80
  237.3 69.9 %reduce-scatter.4.cloned.1.call-start = ((), (), s32[]{:S(2)}) async-start(), calls=%async_computation.6 | async-start | bytes 1474560
  265.4 58.0 %copy-start.4 = (f32[8,6]{1,0:T(8,128)S(1)}, f32[8,6]{1,0:T(8,128)}, u32[]{:S(2)}) copy-start(f32[8,6]{1,0:T(8,128)} %param.21) | copy-start | bytes 580
  309.0 33.2 %all-to-all-start.2 = ((bf16[64,2,640]{2,1,0:T(2,128)(2,1)}), bf16[64,2,640]{2,1,0:T(2,128)(2,1)S(1)}, u32[]{:S(2)}, u32[]{:S(2)}) async-start(bf16[64,2,640]{2,1,0:T(2,128)(2,1)} %reshape.45), calls=%async_computation.2 | async-start | bytes 327680 | tf_op jit(solution)/shard_map/all_to_all | solution.py:88
Sparse Core Ops, SparseCore 0:
  11.9 142.8 all-gather.2
  237.4 24.1 all-gather.4
  267.0 40.1 reduce-scatter.3
where the time goes:
time: 350 us
  waiting for transfers between devices  241 us (69%)
  blocking collectives  51.8 us (15%)
  starting transfers between devices  23.1 us (7%)
  between operations  13.2 us (4%)
  matrix products  12.8 us (4%)
  local copies, waits for them, and re-layouts  6.85 us (2%)
    all_gather x1, waiting for transfers between devices, on_device(): lax.all_gather(flattened, 'expert', axis=0, tiled=True)  143 us
    unnamed x4, waiting for transfers between devices  40.4 us
    psum x1, blocking collectives, on_device(): column_sums = lax.psum(column_terms, 'head')  31.2 us
    all_gather x1, waiting for transfers between devices, on_device(): flat_rows = lax.all_gather(arrived_cols, 'head', axis=1, tiled=True)  24.3 us
    all_to_all x1, blocking collectives, on_device(): lax.all_to_all(outgoing, 'expert', split_axis=0, concat_axis=0, tiled=True)  20.6 us
    all_to_all x1, waiting for transfers between devices, on_device(): lax.all_to_all(summed_rows, 'expert', split_axis=0, concat_axis=0, tiled=...  18.6 us
    all_to_all x1, waiting for transfers between devices, on_device(): lax.all_to_all(column_sums.astype(jnp.bfloat16), 'expert', split_axis=0,...  15.2 us
    all_to_all x1, starting transfers between devices, on_device(): lax.all_to_all(summed_rows, 'expert', split_axis=0, concat_axis=0, tiled=...  14.4 us
  transfers between devices with their start and end apart: 5, of which 5 were waited for; matrix products, arithmetic and copies ran while one was open for 0% of the time, Pallas kernels for 0%

commit v1 on v0

--- a/solution.py
+++ b/solution.py
@@ -77,8 +77,36 @@
     outgoing = outgoing.reshape(expert_count, capacity, -1)
     arrived = lax.all_to_all(outgoing, "expert", split_axis=0, concat_axis=0, tiled=True)
     arrived_cols = arrived.reshape(-1, arrived.shape[2])
-    flat_rows = lax.all_gather(arrived_cols, "head", axis=1, tiled=True)
-    projected = jnp.einsum("rd,gfd->rgf", flat_rows, gate_up, preferred_element_type=jnp.float32)
+
+    def stages_all_save(array_here, array_dim, q_in):
+        left_arr = lax.axis_index("head")
+        local_part = lax.axis_size("head")
+        local_now, w_next, x_next = (local_part, left_arr, array_here.shape[array_dim])
+        so_far_all = tuple(((ii, (ii + 1) % local_now) for ii in range(local_now)))
+        rack = tuple(((ii, (ii - 1) % local_now) for ii in range(local_now)))
+        raw_out = local_now // 2
+        built = e_next = array_here
+        fresh = q_in(array_here, w_next * x_next)
+        for num in range(1, raw_out + 1):
+            built = lax.ppermute(built, "head", so_far_all)
+            if num < local_now - raw_out:
+                e_next = lax.ppermute(e_next, "head", rack)
+                everything = q_in(e_next, (w_next + num) % local_now * x_next)
+                fresh = fresh + everything
+            carry_in = q_in(built, (w_next - num) % local_now * x_next)
+            fresh = fresh + carry_in
+        return fresh
+
+    projected = stages_all_save(
+        arrived_cols,
+        1,
+        lambda part, offset_2: jnp.einsum(
+            "rd,gfd->rgf",
+            part,
+            lax.dynamic_slice_in_dim(gate_up, offset_2, part.shape[1], axis=2),
+            preferred_element_type=jnp.float32,
+        ),
+    )
     hidden = (jax.nn.silu(projected[:, 0]) * projected[:, 1]).astype(jnp.bfloat16)
     partial_rows = jnp.dot(hidden, down_local, preferred_element_type=jnp.float32)
     summed_cols = lax.psum_scatter(

time: 350 us -> 339 us (0.969)
  starting transfers between devices: 23.1 us -> 43.8 us
  blocking collectives: 51.8 us -> 31.2 us
  waiting for transfers between devices: 241 us -> 231 us
    all_gather x1 -> x0, waiting for transfers between devices: 24.3 us -> none  [on_device(): flat_rows = lax.all_gather(arrived_cols, 'head', axis=1, tiled=True)]
    all_to_all x1 -> x0, blocking collectives: 20.6 us -> none  [on_device(): lax.all_to_all(outgoing, 'expert', split_axis=0, concat_axis=0, tiled=True)]
    all_to_all x0 -> x1, waiting for transfers between devices: none -> 15.6 us  [on_device(): lax.all_to_all(outgoing, 'expert', split_axis=0, concat_axis=0, tiled=True)]
    ppermute x0 -> x7, starting transfers between devices: none -> 15.3 us  [the longest x4 11.1 us: stages_all_save(): built = lax.ppermute(built, 'head', so_far_all)]
    unnamed x4 -> x3, waiting for transfers between devices: 40.4 us -> 31.5 us
    ppermute x0 -> x7, waiting for transfers between devices: none -> 7.3 us  [the longest x4 7.28 us: stages_all_save(): built = lax.ppermute(built, 'head', so_far_all)]
    all_to_all x0 -> x1, starting transfers between devices: none -> 5.43 us  [on_device(): lax.all_to_all(outgoing, 'expert', split_axis=0, concat_axis=0, tiled=True)]
  transfers between devices with their start and end apart: 5 -> 12, of which waited for: 5 -> 9; matrix products, arithmetic and copies ran while one was open for 0% -> 1% of each run, Pallas kernels for 0% -> 0%
where the time goes in v1:
time: 339 us
  waiting for transfers between devices  231 us (68%)
  starting transfers between devices  43.8 us (13%)
  blocking collectives  31.2 us (9%)
  between operations  13.8 us (4%)
  matrix products  11.4 us (3%)
  local copies, waits for them, and re-layouts  6.91 us (2%)
    all_gather x1, waiting for transfers between devices, on_device(): lax.all_gather(flattened, 'expert', axis=0, tiled=True)  143 us
    unnamed x3, waiting for transfers between devices  31.5 us
    psum x1, blocking collectives, on_device(): column_sums = lax.psum(column_terms, 'head')  31.2 us
    all_to_all x1, waiting for transfers between devices, on_device(): lax.all_to_all(summed_rows, 'expert', split_axis=0, concat_axis=0, tiled=...  18.5 us
    all_to_all x1, waiting for transfers between devices, on_device(): lax.all_to_all(outgoing, 'expert', split_axis=0, concat_axis=0, tiled=True)  15.6 us
    all_to_all x1, waiting for transfers between devices, on_device(): lax.all_to_all(column_sums.astype(jnp.bfloat16), 'expert', split_axis=0,...  15.2 us
    all_to_all x1, starting transfers between devices, on_device(): lax.all_to_all(summed_rows, 'expert', split_axis=0, concat_axis=0, tiled=...  14.4 us
    ppermute x4, starting transfers between devices, stages_all_save(): built = lax.ppermute(built, 'head', so_far_all)  11.1 us
  transfers between devices with their start and end apart: 12, of which 9 were waited for; matrix products, arithmetic and copies ran while one was open for 1% of the time, Pallas kernels for 0%

profile of v1, /device:TPU:7, one launch (start us, length us, event | category | flops | bytes accessed | tf_op | source)
XLA Modules:
  0.0 338.6 jit_solution(9450689252572971010)
XLA Ops:
  6.5 1.8 fusion.54
  8.3 1.1 fusion.7
  9.6 1.5 fusion.3
  12.3 142.5 %all-gather.2.cloned.1.call-done = bf16[512,4096]{1,0:T(8,128)(2,1)} async-done(((bf16[8,4096]{1,0:T(8,128)(2,1)}), bf16[512,4096]{1,0:T(8,128)(2,1)}) %all-gather.2.cloned.1.call-update) | async-done | bytes 4194320 | tf_op jit(solution)/shard_map/all_gather | solution.py:44
  154.8 3.6 %fusion.55 = f32[512,80]{0,1:T(8,128)S(1)} fusion(bf16[512,4096]{1,0:T(8,128)(2,1)} %all-gather.2.cloned.1.call-done, bf16[4096,80]{0,1:T(8,128)(2,1)S(1)} %copy-done.2), kind=kOutput, calls=%fused_computation.78 | convolution fusion | flops 335544320 | bytes 5013504 | tf_op jit(solution)/shard_map/dot_general | solution.py:43
  158.4 31.2 %all-reduce.1 = bf16[512,80]{0,1:T(8,128)(2,1)S(1)} all-reduce(f32[512,80]{0,1:T(8,128)S(1)} %fusion.55), channel_id=1, replica_groups=mesh['head'=8,'expert'=64] {'head'}, use_global_device_ids=true, to_apply=%region_2.3 | all-reduce | flops 40960 | bytes 245760 | tf_op jit(solution)/shard_map/psum | solution.py:48
  190.4 8.6 %all-to-all-start = ((bf16[64,8,80]{2,1,0:T(8,128)(2,1)}), bf16[64,8,80]{2,1,0:T(8,128)(2,1)S(1)}, u32[]{:S(2)}, u32[]{:S(2)}) async-start(bf16[64,8,80]{2,1,0:T(8,128)(2,1)} %bitcast), calls=%async_computation | async-start | bytes 262144 | tf_op jit(solution)/shard_map/all_to_all | solution.py:49
  199.9 15.2 %all-to-all-done = bf16[64,8,80]{2,1,0:T(8,128)(2,1)S(1)} async-done(((bf16[64,8,80]{2,1,0:T(8,128)(2,1)}), bf16[64,8,80]{2,1,0:T(8,128)(2,1)S(1)}, u32[]{:S(2)}, u32[]{:S(2)}) %all-to-all-start) | async-done | bytes 81952 | tf_op jit(solution)/shard_map/all_to_all | solution.py:49
  216.6 5.4 %all-to-all-start.1 = ((bf16[64,2,640]{2,1,0:T(2,128)(2,1)}), bf16[64,2,640]{2,1,0:T(2,128)(2,1)S(1)}, u32[]{:S(2)}, u32[]{:S(2)}) async-start(bf16[64,2,640]{2,1,0:T(2,128)(2,1)} %reshape.51), calls=%async_computation.1 | async-start | bytes 327680 | tf_op jit(solution)/shard_map/all_to_all | solution.py:78
  222.2 15.6 %all-to-all-done.1 = bf16[64,2,640]{2,1,0:T(2,128)(2,1)S(1)} async-done(((bf16[64,2,640]{2,1,0:T(2,128)(2,1)}), bf16[64,2,640]{2,1,0:T(2,128)(2,1)S(1)}, u32[]{:S(2)}, u32[]{:S(2)}) %all-to-all-start.1) | async-done | bytes 163872 | tf_op jit(solution)/shard_map/all_to_all | solution.py:78
  237.9 4.2 %collective-permute-start = (bf16[128,640]{1,0:T(8,128)(2,1)S(1)}, bf16[128,640]{1,0:T(8,128)(2,1)S(1)}, u32[]{:S(2)}, u32[]{:S(2)}) collective-permute-start(bf16[128,640]{1,0:T(8,128)(2,1)S(1)} %reshape.52), channel_id=1, source_target_pairs={{0,448},{64,0},{128,64},{192,128},{256,192},{320,256},{384,320},{4... | collective-permute-start | bytes 491528 | tf_op jit(solution)/shard_map/ppermute | solution.py:93
  242.4 2.0 collective-permute-done.1
  244.4 3.7 %collective-permute-start.3 = (bf16[128,640]{1,0:T(8,128)(2,1)S(1)}, bf16[128,640]{1,0:T(8,128)(2,1)S(1)}, u32[]{:S(2)}, u32[]{:S(2)}) collective-permute-start(bf16[128,640]{1,0:T(8,128)(2,1)S(1)} %collective-permute-done.1), channel_id=1, source_target_pairs={{0,64},{64,128},{128,192},{192,256},{256,320},{320,384},{384,448},... | collective-permute-start | bytes 491528 | tf_op jit(solution)/shard_map/ppermute | solution.py:91
  248.5 1.8 collective-permute-done.3
  250.3 3.7 %collective-permute-start.5 = (bf16[128,640]{1,0:T(8,128)(2,1)S(1)}, bf16[128,640]{1,0:T(8,128)(2,1)S(1)}, u32[]{:S(2)}, u32[]{:S(2)}) collective-permute-start(bf16[128,640]{1,0:T(8,128)(2,1)S(1)} %collective-permute-done.3), channel_id=1, source_target_pairs={{0,64},{64,128},{128,192},{192,256},{256,320},{320,384},{384,448},... | collective-permute-start | bytes 491528 | tf_op jit(solution)/shard_map/ppermute | solution.py:91
  254.5 1.8 collective-permute-done.5
  256.3 3.7 %collective-permute-start.6 = (bf16[128,640]{1,0:T(8,128)(2,1)S(1)}, bf16[128,640]{1,0:T(8,128)(2,1)S(1)}, u32[]{:S(2)}, u32[]{:S(2)}) collective-permute-start(bf16[128,640]{1,0:T(8,128)(2,1)S(1)} %collective-permute-done.5), channel_id=1, source_target_pairs={{0,64},{64,128},{128,192},{192,256},{256,320},{320,384},{384,448},... | collective-permute-start | bytes 491528 | tf_op jit(solution)/shard_map/ppermute | solution.py:91
  260.5 1.8 collective-permute-done.6
  263.0 1.5 copy.22
  264.5 31.5 %reduce-scatter.4.cloned.1.call-done = bf16[640,128]{1,0:T(8,128)(2,1)} async-done(((bf16[5120,128]{1,0:T(8,128)(2,1)}), bf16[640,128]{1,0:T(8,128)(2,1)}) %reduce-scatter.4.cloned.1.call-update) | async-done | bytes 163856
  296.0 1.1 copy.23
  297.8 14.4 %all-to-all-start.2 = ((bf16[64,2,640]{2,1,0:T(2,128)(2,1)}), bf16[64,2,640]{2,1,0:T(2,128)(2,1)S(1)}, u32[]{:S(2)}, u32[]{:S(2)}) async-start(bf16[64,2,640]{2,1,0:T(2,128)(2,1)} %reshape.53), calls=%async_computation.2 | async-start | bytes 327680 | tf_op jit(solution)/shard_map/all_to_all | solution.py:116
  312.4 18.5 %all-to-all-done.2 = bf16[64,2,640]{2,1,0:T(2,128)(2,1)S(1)} async-done(((bf16[64,2,640]{2,1,0:T(2,128)(2,1)}), bf16[64,2,640]{2,1,0:T(2,128)(2,1)S(1)}, u32[]{:S(2)}, u32[]{:S(2)}) %all-to-all-start.2) | async-done | bytes 163872 | tf_op jit(solution)/shard_map/all_to_all | solution.py:116
  331.0 0.8 convolution_add_fusion.6
  (56 shorter events, 8.0 us)
Async XLA Ops:
  6.5 235.6 %copy-start = (bf16[1,2,96,5120]{3,2,1,0:T(8,128)(2,1)S(1)}, bf16[1,2,96,5120]{3,2,1,0:T(8,128)(2,1)}, u32[]{:S(2)}) copy-start(bf16[1,2,96,5120]{3,2,1,0:T(8,128)(2,1)} %param.22) | copy-start | bytes 5898244
  6.5 5.3 %copy-start.4 = (s32[8,6]{1,0:T(8,128)S(1)}, s32[8,6]{1,0:T(8,128)}, u32[]{:S(2)}) copy-start(s32[8,6]{1,0:T(8,128)} %param.20) | copy-start | bytes 580
  6.5 148.3 %copy-start.2 = (bf16[4096,80]{0,1:T(8,128)(2,1)S(1)}, bf16[4096,80]{0,1:T(8,128)(2,1)}, u32[]{:S(2)}) copy-start(bf16[4096,80]{0,1:T(8,128)(2,1)} %param.17) | copy-start | bytes 1966084
  6.5 148.3 %all-gather.2.cloned.1.call-start = ((), (), s32[]{:S(2)}) async-start(), calls=%async_computation.4 | async-start | bytes 4259840 | tf_op jit(solution)/shard_map/all_gather | solution.py:44
  158.4 57.0 %copy-start.3 = (bf16[8,5120]{1,0:T(8,128)(2,1)S(1)}, bf16[8,5120]{1,0:T(8,128)(2,1)}, u32[]{:S(2)}) copy-start(bf16[8,5120]{1,0:T(8,128)(2,1)} %param.18) | copy-start | bytes 245764
  190.4 24.8 %all-to-all-start = ((bf16[64,8,80]{2,1,0:T(8,128)(2,1)}), bf16[64,8,80]{2,1,0:T(8,128)(2,1)S(1)}, u32[]{:S(2)}, u32[]{:S(2)}) async-start(bf16[64,8,80]{2,1,0:T(8,128)(2,1)} %bitcast), calls=%async_computation | async-start | bytes 262144 | tf_op jit(solution)/shard_map/all_to_all | solution.py:49
  216.6 21.2 %all-to-all-start.1 = ((bf16[64,2,640]{2,1,0:T(2,128)(2,1)}), bf16[64,2,640]{2,1,0:T(2,128)(2,1)S(1)}, u32[]{:S(2)}, u32[]{:S(2)}) async-start(bf16[64,2,640]{2,1,0:T(2,128)(2,1)} %reshape.51), calls=%async_computation.1 | async-start | bytes 327680 | tf_op jit(solution)/shard_map/all_to_all | solution.py:78
  222.0 73.9 %reduce-scatter.4.cloned.1.call-start = ((), (), s32[]{:S(2)}) async-start(), calls=%async_computation.5 | async-start | bytes 1474560
  237.9 10.2 %collective-permute-start = (bf16[128,640]{1,0:T(8,128)(2,1)S(1)}, bf16[128,640]{1,0:T(8,128)(2,1)S(1)}, u32[]{:S(2)}, u32[]{:S(2)}) collective-permute-start(bf16[128,640]{1,0:T(8,128)(2,1)S(1)} %reshape.52), channel_id=1, source_target_pairs={{0,448},{64,0},{128,64},{192,128},{256,192},{320,256},{384,320},{4... | collective-permute-start | bytes 491528 | tf_op jit(solution)/shard_map/ppermute | solution.py:93
  242.1 2.3 collective-permute-start.1
  244.4 6.0 %collective-permute-start.3 = (bf16[128,640]{1,0:T(8,128)(2,1)S(1)}, bf16[128,640]{1,0:T(8,128)(2,1)S(1)}, u32[]{:S(2)}, u32[]{:S(2)}) collective-permute-start(bf16[128,640]{1,0:T(8,128)(2,1)S(1)} %collective-permute-done.1), channel_id=1, source_target_pairs={{0,64},{64,128},{128,192},{192,256},{256,320},{320,384},{384,448},... | collective-permute-start | bytes 491528 | tf_op jit(solution)/shard_map/ppermute | solution.py:91
  248.1 6.2 %collective-permute-start.2 = (bf16[128,640]{1,0:T(8,128)(2,1)S(1)}, bf16[128,640]{1,0:T(8,128)(2,1)S(1)}, u32[]{:S(2)}, u32[]{:S(2)}) collective-permute-start(bf16[128,640]{1,0:T(8,128)(2,1)S(1)} %collective-permute-done), channel_id=1, source_target_pairs={{0,448},{64,0},{128,64},{192,128},{256,192},{320,256},{384,320},{4... | collective-permute-start | bytes 491528 | tf_op jit(solution)/shard_map/ppermute | solution.py:93
  248.3 14.2 %copy-start.1 = (bf16[1,96,5120]{2,1,0:T(8,128)(2,1)S(1)}, bf16[1,96,5120]{2,1,0:T(8,128)(2,1)}, u32[]{:S(2)}) copy-start(bf16[1,96,5120]{2,1,0:T(8,128)(2,1)} %param.23) | copy-start | bytes 2949124
  250.3 6.0 %collective-permute-start.5 = (bf16[128,640]{1,0:T(8,128)(2,1)S(1)}, bf16[128,640]{1,0:T(8,128)(2,1)S(1)}, u32[]{:S(2)}, u32[]{:S(2)}) collective-permute-start(bf16[128,640]{1,0:T(8,128)(2,1)S(1)} %collective-permute-done.3), channel_id=1, source_target_pairs={{0,64},{64,128},{128,192},{192,256},{256,320},{320,384},{384,448},... | collective-permute-start | bytes 491528 | tf_op jit(solution)/shard_map/ppermute | solution.py:91
  254.3 6.0 %collective-permute-start.4 = (bf16[128,640]{1,0:T(8,128)(2,1)S(1)}, bf16[128,640]{1,0:T(8,128)(2,1)S(1)}, u32[]{:S(2)}, u32[]{:S(2)}) collective-permute-start(bf16[128,640]{1,0:T(8,128)(2,1)S(1)} %collective-permute-done.2), channel_id=1, source_target_pairs={{0,448},{64,0},{128,64},{192,128},{256,192},{320,256},{384,320},{4... | collective-permute-start | bytes 491528 | tf_op jit(solution)/shard_map/ppermute | solution.py:93
  256.3 6.0 %collective-permute-start.6 = (bf16[128,640]{1,0:T(8,128)(2,1)S(1)}, bf16[128,640]{1,0:T(8,128)(2,1)S(1)}, u32[]{:S(2)}, u32[]{:S(2)}) collective-permute-start(bf16[128,640]{1,0:T(8,128)(2,1)S(1)} %collective-permute-done.5), channel_id=1, source_target_pairs={{0,64},{64,128},{128,192},{192,256},{256,320},{320,384},{384,448},... | collective-permute-start | bytes 491528 | tf_op jit(solution)/shard_map/ppermute | solution.py:91
  263.0 49.2 %copy-start.5 = (f32[8,6]{1,0:T(8,128)S(1)}, f32[8,6]{1,0:T(8,128)}, u32[]{:S(2)}) copy-start(f32[8,6]{1,0:T(8,128)} %param.21) | copy-start | bytes 580
  297.8 33.1 %all-to-all-start.2 = ((bf16[64,2,640]{2,1,0:T(2,128)(2,1)}), bf16[64,2,640]{2,1,0:T(2,128)(2,1)S(1)}, u32[]{:S(2)}, u32[]{:S(2)}) async-start(bf16[64,2,640]{2,1,0:T(2,128)(2,1)} %reshape.53), calls=%async_computation.2 | async-start | bytes 327680 | tf_op jit(solution)/shard_map/all_to_all | solution.py:116
Sparse Core Ops, SparseCore 0:
  11.9 142.8 all-gather.1
  264.6 31.3 reduce-scatter.3
